TPU v7x, 32 devices: a whole 2x2x4 slice. The times are simulated.
32 devices in a mesh: space: 4 (over z), dp: 8 (over y, x, core).
Axes of the slice: x: 2, y: 2, z: 4, core: 2. Of those that a mesh axis runs over, the one named last changes fastest.
Arguments:
- features: bfloat16 [8, 12, 128, 320], P('dp', 'space'), may hold values from -6 to 6
- cotangent: bfloat16 [8, 12, 128, 320], P('dp', 'space'), may hold values from -6 to 6
- norm_gain: float32 [320], replicated, may hold values from 0.1 to 1.9
- norm_bias: float32 [320], replicated, may hold values from -0.5 to 0.5
- weight: bfloat16 [2880, 320], P('dp'), may hold values from -0.109375 to 0.109375
- moment_one: float32 [2880, 320], P('dp'), may hold values from -332.55374 to 332.55374
- moment_two: float32 [2880, 320], P('dp'), may hold values from 768 to 6144
- heights: int32 [8], P('dp'), may hold values from 6 to 12, as said below
- widths: int32 [8], P('dp'), may hold values from 64 to 128, as said below
Outputs:
- block_out: bfloat16 [8, 12, 128, 320], P('dp', 'space')
- input_grad: bfloat16 [8, 12, 128, 320], P('dp', 'space')
- weight_grad: float32 [2880, 320], P('dp')
- adam_update: float32 [2880, 320], P('dp')
Inputs may be any that keep to these rules, and one draw needn't show every extreme that they name: Image i occupies canvas rows 0 to heights[i] - 1; some image has all 12 rows. Image i occupies canvas columns 0 to widths[i] - 1; some image has all 128 columns.
All inputs are finite; a program needn't handle non-finite values.
Results may differ from a plain program's by a relative error of at most 0.017.
Values may be sent and summed in bfloat16 or wider, within the bound.
No kernel may reach another device: no remote copies, remote signals or barrier semaphores. Data moves between devices by JAX's collectives and lax.ppermute only.
A program may use at most 64 MiB of HBM per device.

v0:
```python
import jax
import jax.numpy as jnp
from jax import lax
from jax.sharding import PartitionSpec as P

GROUPS = 32


def with_halo(cells, sides, width):
    for axis, dim in sides:
        count = lax.axis_size(axis)
        ends = count - 1
        head = lax.slice_in_dim(cells, 0, width, axis=dim)
        tail = lax.slice_in_dim(cells, cells.shape[dim] - width, cells.shape[dim], axis=dim)
        cells = jnp.concatenate(
            [
                lax.ppermute(tail, axis, [(i, (i + 1) % count) for i in range(ends)]),
                cells,
                lax.ppermute(head, axis, [((i + 1) % count, i) for i in range(ends)]),
            ],
            axis=dim,
        )
    return cells


def group_sum(values, groups):
    height_dev, width_dev, channels = values.shape
    return values.reshape(height_dev, width_dev, groups, channels // groups).sum(axis=(0, 1, 3))


def spread_groups(statistic, channels):
    return jnp.repeat(statistic, channels // statistic.shape[0])


def pad_columns(padded_rows):
    return jnp.pad(padded_rows, ((0, 0), (1, 1), (0, 0)))


def local(
    features, cotangent, norm_gain, norm_bias, weight, moment_one, moment_two, heights, widths
):
    latent = features[0]
    height_dev, width_dev, channels = latent.shape
    row_ids = lax.axis_index("space") * height_dev + jnp.arange(height_dev, dtype=jnp.int32)
    inside = (
        (row_ids < heights[0])[:, None]
        & (jnp.arange(width_dev, dtype=jnp.int32) < widths[0])[None, :]
    ).astype(jnp.float32)[..., None]
    cell_count = (heights[0] * widths[0] * (channels // GROUPS)).astype(jnp.float32)
    gathered = lax.all_gather(weight, "dp", axis=0, tiled=True)
    tap_weights = gathered.reshape(9, channels, channels)
    values = latent.astype(jnp.float32) * inside
    group_total, squares = lax.psum(
        (group_sum(values, GROUPS), group_sum(values * values, GROUPS)), "space"
    )
    center = group_total / cell_count
    spread = squares / cell_count - center * center
    inverse = lax.rsqrt(spread + 1e-05)
    normed = (values - spread_groups(center, channels)) * spread_groups(inverse, channels) * inside
    before = normed * norm_gain + norm_bias
    activated = (jax.nn.silu(before) * inside).astype(jnp.bfloat16)
    act_pad = pad_columns(with_halo(activated, (("space", 0),), 1))
    output = jnp.zeros((height_dev * width_dev, channels), jnp.float32)
    for row_off in range(3):
        for col_off in range(3):
            window = act_pad[row_off : row_off + height_dev, col_off : col_off + width_dev].reshape(
                -1, channels
            )
            output = output + jnp.dot(
                window, tap_weights[row_off * 3 + col_off], preferred_element_type=jnp.float32
            )
    block_out = (output.reshape(height_dev, width_dev, channels) * inside).astype(jnp.bfloat16)
    masked = cotangent[0] * inside.astype(jnp.bfloat16)
    cot_pad = pad_columns(with_halo(masked, (("space", 0),), 1))
    flat_cot = masked.reshape(-1, channels)
    upstream = jnp.zeros((height_dev * width_dev, channels), jnp.float32)
    tap_grads = []
    for row_off in range(3):
        for col_off in range(3):
            tap_index = row_off * 3 + col_off
            window = act_pad[row_off : row_off + height_dev, col_off : col_off + width_dev].reshape(
                -1, channels
            )
            tap_grads.append(
                lax.dot_general(
                    window, flat_cot, (((0,), (0,)), ((), ())), preferred_element_type=jnp.float32
                )
            )
            cot_window = cot_pad[
                2 - row_off : 2 - row_off + height_dev, 2 - col_off : 2 - col_off + width_dev
            ].reshape(-1, channels)
            upstream = upstream + lax.dot_general(
                cot_window,
                tap_weights[tap_index],
                (((1,), (1,)), ((), ())),
                preferred_element_type=jnp.float32,
            )
    weight_terms = jnp.stack(tap_grads).reshape(9 * channels, channels)
    gate_sig = jax.nn.sigmoid(before)
    silu_slope = gate_sig * (1.0 + before * (1.0 - gate_sig))
    scaled = upstream.reshape(height_dev, width_dev, channels) * silu_slope * inside * norm_gain
    local_first = group_sum(scaled, GROUPS)
    local_second = group_sum(scaled * normed, GROUPS)
    grad_piece = lax.psum_scatter(weight_terms, "dp", scatter_dimension=0, tiled=True)
    sum_first, sum_second = lax.psum((local_first, local_second), "space")
    grad_piece = lax.psum(grad_piece.astype(jnp.bfloat16), "space").astype(jnp.float32)
    first = sum_first / cell_count
    second = sum_second / cell_count
    input_grad = (
        spread_groups(inverse, channels)
        * (scaled - spread_groups(first, channels) - normed * spread_groups(second, channels))
        * inside
    ).astype(jnp.bfloat16)
    first_new = 0.9 * moment_one + 0.1 * grad_piece
    second_new = 0.999 * moment_two + 0.001 * grad_piece * grad_piece
    adam_update = first_new / (1.0 - 0.9**10) / (jnp.sqrt(second_new / (1.0 - 0.999**10)) + 1e-08)
    return (block_out[None], input_grad[None], grad_piece, adam_update)


def solution(mesh):
    placed = (
        P("dp", "space", None, None),
        P("dp", "space", None, None),
        P(),
        P(),
        P("dp", None),
        P("dp", None),
        P("dp", None),
        P("dp"),
        P("dp"),
    )
    return jax.shard_map(
        local,
        mesh=mesh,
        in_specs=placed,
        out_specs=(
            P("dp", "space", None, None),
            P("dp", "space", None, None),
            P("dp", None),
            P("dp", None),
        ),
        check_vma=False,
    )
```

profile of v0, /device:TPU:0, one launch (start us, length us, event | category | flops | bytes accessed | tf_op | source)
XLA Modules:
  0.0 207.1 jit_solution(10719719046943289507)
XLA Ops:
  9.4 1.1 multiply_reduce_fusion.1
  11.0 13.5 %all-reduce.4 = (f32[32]{0:T(128)S(1)}, f32[32]{0:T(128)S(1)}) all-reduce(f32[32]{0:T(128)S(1)} %reduce_sum.51, f32[32]{0:T(128)S(1)} %reduce_sum.54), channel_id=1, replica_groups=mesh['space'=4,'dp'=8] {'space'}, use_global_device_ids=true, to_apply=%region_2.0 | all-reduce | flops 64 | bytes 512 | tf_op jit(solution)/shard_map/psum | solution.py:53
  24.9 1.3 multiply_convert_fusion.4
  26.2 1.3 collective-permute-start
  27.5 1.3 collective-permute-start.1
  29.8 1.2 dynamic-slice
  31.7 2.1 %collective-permute-done.1 = bf16[1,128,320]{1,2,0:T(8,128)(2,1)S(1)} collective-permute-done((bf16[1,128,320]{1,2,0:T(8,128)(2,1)S(1)}, bf16[1,128,320]{1,2,0:T(8,128)(2,1)S(1)}, u32[]{:S(2)}, u32[]{:S(2)}) %collective-permute-start.1) | collective-permute-done | bytes 81952 | tf_op jit(solution)/shard_map/ppermute | solution.py:19
  34.3 1.1 fusion.9
  35.4 1.1 fusion.2
  36.5 1.2 fusion.8
  38.7 1.3 fusion.6
  40.0 1.2 fusion.5
  41.2 1.1 fusion.4
  42.3 1.1 fusion.1
  43.4 1.1 fusion.3
  44.5 5.6 %copy.68 = f32[2880,320]{0,1:T(8,128)} copy(f32[2880,320]{1,0:T(8,128)} %bitcast.48) | data formatting | bytes 7372800 | tf_op jit(solution)/shard_map/reshape | solution.py:98
  50.2 80.3 %all-reduce.9 = bf16[2880,320]{0,1:T(8,128)(2,1)S(1)} all-reduce(f32[2880,320]{0,1:T(8,128)} %copy.68), channel_id=2, replica_groups=mesh['space'=4,'dp'=8] {'dp'}, use_global_device_ids=true, to_apply=%region_12.13.clone | all-reduce | flops 921600 | bytes 5529600
  132.6 2.7 %collective-permute-start.2 = (bf16[1,128,320]{1,2,0:T(8,128)(2,1)}, bf16[1,128,320]{1,2,0:T(8,128)(2,1)S(1)}, u32[]{:S(2)}, u32[]{:S(2)}) collective-permute-start(bf16[1,128,320]{1,2,0:T(8,128)(2,1)} %get-tuple-element.30), channel_id=1, source_target_pairs={{0,8},{8,16},{16,24},{1,9},{9,17},{17,25},{2,10},{10,18},{18,26},{... | collective-permute-start | bytes 245768 | tf_op jit(solution)/shard_map/ppermute | solution.py:17
  135.2 1.5 collective-permute-start.3
  136.9 1.2 copy.60
  139.3 1.1 fusion.84
  140.4 1.2 copy.43
  149.0 1.9 copy.57
  156.3 8.3 %all-reduce.8.cloned.1.call-done = bf16[360,320]{0,1:T(8,128)(2,1)} async-done(((bf16[360,320]{0,1:T(8,128)(2,1)}), bf16[360,320]{0,1:T(8,128)(2,1)}) %all-reduce.8.cloned.1.call-update) | async-done | bytes 230416 | tf_op jit(solution)/shard_map/psum | solution.py:106
  164.5 2.5 %fusion.17 = (f32[360,320]{0,1:T(8,128)}, f32[360,320]{0,1:T(8,128)}) fusion(f32[360,320]{0,1:T(8,128)} %param.15, f32[360,320]{0,1:T(8,128)} %param.14, bf16[360,320]{0,1:T(8,128)(2,1)} %all-reduce.8.cloned.1.call-done), kind=kLoop, calls=%fused_computation.47 | loop fusion | flops 1382400 | bytes 2073600 | tf_op jit(solution)/shard_map/div | solution.py:116
  167.0 3.9 %copy.44 = bf16[8,360,320]{1,0,2:T(8,128)(2,1)} copy(bf16[8,360,320]{1,2,0:T(8,128)(2,1)} %all-gather.3.cloned.1.call-done) | data formatting | bytes 3686400 | tf_op jit(solution)/shard_map/all_gather | solution.py:50
  170.9 3.4 %reshape.284 = bf16[2880,320]{0,1:T(8,128)(2,1)S(1)} reshape(bf16[8,360,320]{1,0,2:T(8,128)(2,1)} %copy.44) | data formatting | bytes 3686400
  174.7 1.3 fusion.50
  179.6 1.4 fusion.63
  181.0 1.5 convolution_add_fusion.8
  186.7 10.8 %all-reduce.3 = (f32[32]{0:T(128)S(1)}, f32[32]{0:T(128)S(1)}) all-reduce(f32[32]{0:T(128)S(1)} %reduce_sum.75, f32[32]{0:T(128)S(1)} %reduce_sum.72), channel_id=1, replica_groups=mesh['space'=4,'dp'=8] {'space'}, use_global_device_ids=true, to_apply=%region_11.12 | all-reduce | flops 64 | bytes 512 | tf_op jit(solution)/shard_map/psum | solution.py:105
  198.4 1.3 multiply_convert_fusion.1
  (118 shorter events, 28.3 us)
Async XLA Ops:
  8.0 156.5 %all-reduce.8.cloned.1.call-start = ((), (), s32[]{:S(2)}) async-start(), calls=%async_computation | async-start | bytes 491520 | tf_op jit(solution)/shard_map/psum | solution.py:106
  26.2 5.5 %collective-permute-start = (bf16[1,128,320]{1,2,0:T(8,128)(2,1)S(1)}, bf16[1,128,320]{1,2,0:T(8,128)(2,1)S(1)}, u32[]{:S(2)}, u32[]{:S(2)}) collective-permute-start(bf16[1,128,320]{1,2,0:T(8,128)(2,1)S(1)} %get-tuple-element.34), channel_id=1, source_target_pairs={{0,8},{8,16},{16,24},{1,9},{9,17},{17,25},{2,10},{10,18},{18,26},{... | collective-permute-start | bytes 245768 | tf_op jit(solution)/shard_map/ppermute | solution.py:17
  27.5 6.3 %collective-permute-start.1 = (bf16[1,128,320]{1,2,0:T(8,128)(2,1)S(1)}, bf16[1,128,320]{1,2,0:T(8,128)(2,1)S(1)}, u32[]{:S(2)}, u32[]{:S(2)}) collective-permute-start(bf16[1,128,320]{1,2,0:T(8,128)(2,1)S(1)} %get-tuple-element.35), channel_id=1, source_target_pairs={{8,0},{16,8},{24,16},{9,1},{17,9},{25,17},{10,2},{18,10},{26,18},{... | collective-permute-start | bytes 245768 | tf_op jit(solution)/shard_map/ppermute | solution.py:19
  31.7 6.0 %copy-start.12 = (bf16[1,128,320]{1,2,0:T(8,128)(2,1)}, bf16[1,128,320]{1,2,0:T(8,128)(2,1)S(1)}, u32[]{:S(2)}) copy-start(bf16[1,128,320]{1,2,0:T(8,128)(2,1)S(1)} %collective-permute-done) | copy-start | bytes 245764
  33.8 8.5 %copy-start.14 = (bf16[1,128,320]{1,2,0:T(8,128)(2,1)}, bf16[1,128,320]{1,2,0:T(8,128)(2,1)S(1)}, u32[]{:S(2)}) copy-start(bf16[1,128,320]{1,2,0:T(8,128)(2,1)S(1)} %collective-permute-done.1) | copy-start | bytes 245764
  34.2 4.5 %copy-start = (bf16[1,3,128,320]{2,3,1,0:T(8,128)(2,1)S(1)}, bf16[1,3,128,320]{2,3,1,0:T(8,128)(2,1)}, u32[]{:S(2)}) copy-start(bf16[1,3,128,320]{2,3,1,0:T(8,128)(2,1)} %param.9) | copy-start | bytes 737284
  34.2 4.5 %copy-start.10 = (bf16[1,3,128,320]{2,3,1,0:T(8,128)(2,1)S(1)}, bf16[1,3,128,320]{2,3,1,0:T(8,128)(2,1)}, u32[]{:S(2)}) copy-start(bf16[1,3,128,320]{2,3,1,0:T(8,128)(2,1)} %param.10) | copy-start | bytes 737284
  34.2 4.5 %copy-start.19 = (f32[320]{0:T(512)S(1)}, f32[320]{0:T(512)}, u32[]{:S(2)}) copy-start(f32[320]{0:T(512)} %param.12) | copy-start | bytes 3844
  34.2 4.5 %copy-start.20 = (f32[320]{0:T(512)S(1)}, f32[320]{0:T(512)}, u32[]{:S(2)}) copy-start(f32[320]{0:T(512)} %param.11) | copy-start | bytes 3844
  131.3 35.7 %all-gather.3.cloned.1.call-start = ((), (), s32[]{:S(2)}) async-start(), calls=%async_computation.1 | async-start | bytes 2211840 | tf_op jit(solution)/shard_map/all_gather | solution.py:50
  132.6 14.1 %collective-permute-start.2 = (bf16[1,128,320]{1,2,0:T(8,128)(2,1)}, bf16[1,128,320]{1,2,0:T(8,128)(2,1)S(1)}, u32[]{:S(2)}, u32[]{:S(2)}) collective-permute-start(bf16[1,128,320]{1,2,0:T(8,128)(2,1)} %get-tuple-element.30), channel_id=1, source_target_pairs={{0,8},{8,16},{16,24},{1,9},{9,17},{17,25},{2,10},{10,18},{18,26},{... | collective-permute-start | bytes 245768 | tf_op jit(solution)/shard_map/ppermute | solution.py:17
  135.2 11.4 %collective-permute-start.3 = (bf16[1,128,320]{1,2,0:T(8,128)(2,1)}, bf16[1,128,320]{1,2,0:T(8,128)(2,1)S(1)}, u32[]{:S(2)}, u32[]{:S(2)}) collective-permute-start(bf16[1,128,320]{1,2,0:T(8,128)(2,1)} %get-tuple-element.31), channel_id=1, source_target_pairs={{8,0},{16,8},{24,16},{9,1},{17,9},{25,17},{10,2},{18,10},{26,18},{... | collective-permute-start | bytes 245768 | tf_op jit(solution)/shard_map/ppermute | solution.py:19
  139.3 2.3 %copy-start.13 = (bf16[1,128,320]{1,2,0:T(8,128)(2,1)S(1)}, bf16[1,128,320]{1,2,0:T(8,128)(2,1)}, u32[]{:S(2)}) copy-start(bf16[1,128,320]{1,2,0:T(8,128)(2,1)} %copy-done.12) | copy-start | bytes 245764
  139.3 2.3 %copy-start.15 = (bf16[1,128,320]{1,2,0:T(8,128)(2,1)S(1)}, bf16[1,128,320]{1,2,0:T(8,128)(2,1)}, u32[]{:S(2)}) copy-start(bf16[1,128,320]{1,2,0:T(8,128)(2,1)} %copy-done.14) | copy-start | bytes 245764
  140.4 2.2 %copy-start.11 = (bf16[3,128,320]{1,2,0:T(8,128)(2,1)S(1)}, bf16[3,128,320]{1,2,0:T(8,128)(2,1)}, u32[]{:S(2)}) copy-start(bf16[3,128,320]{1,2,0:T(8,128)(2,1)} %get-tuple-element.26) | copy-start | bytes 737284
  174.3 1.7 copy-start.7
  174.3 2.1 %copy-start.3 = (bf16[3,128,320]{2,1,0:T(8,128)(2,1)S(1)}, bf16[3,128,320]{2,1,0:T(8,128)(2,1)}, u32[]{:S(2)}) copy-start(bf16[3,128,320]{2,1,0:T(8,128)(2,1)} %copy.45) | copy-start | bytes 737284
  174.7 2.2 %copy-start.2 = (bf16[3,128,320]{2,1,0:T(8,128)(2,1)S(1)}, bf16[3,128,320]{2,1,0:T(8,128)(2,1)}, u32[]{:S(2)}) copy-start(bf16[3,128,320]{2,1,0:T(8,128)(2,1)} %copy.46) | copy-start | bytes 737284
  176.0 1.1 copy-start.1
  176.8 1.1 copy-start.16
  179.6 2.9 %copy-start.9 = (bf16[3,128,320]{2,1,0:T(8,128)(2,1)S(1)}, bf16[3,128,320]{2,1,0:T(8,128)(2,1)}, u32[]{:S(2)}) copy-start(bf16[3,128,320]{2,1,0:T(8,128)(2,1)} %copy.58) | copy-start | bytes 737284
  179.6 3.3 %copy-start.8 = (bf16[3,128,320]{2,1,0:T(8,128)(2,1)S(1)}, bf16[3,128,320]{2,1,0:T(8,128)(2,1)}, u32[]{:S(2)}) copy-start(bf16[3,128,320]{2,1,0:T(8,128)(2,1)} %copy.59) | copy-start | bytes 737284
  182.9 1.0 copy-start.6
  183.5 1.0 copy-start.4
  183.9 1.0 copy-start.5
  184.4 1.1 copy-start.17
  184.4 1.1 copy-start.18
Sparse Core Ops, SparseCore 0:
  131.4 33.0 all-reduce.7
Sparse Core Ops, SparseCore 1:
  133.7 24.6 all-gather.2
where the time goes:
time: 208 us; the launch traced here: 207 us
  blocking collectives  105 us (50%)
  local copies, waits for them, and re-layouts  36.4 us (18%)
  matrix products  20.9 us (10%)
  between operations  18 us (9%)
  waiting for transfers between devices  10.9 us (5%)
  other arithmetic  9.44 us (5%)
  starting transfers between devices  6.8 us (3%)
    unnamed x1, blocking collectives  80.3 us
    psum x1, blocking collectives, local(): lax.psum((group_sum(values, GROUPS), group_sum(values * values, GROUPS)),...  13.5 us
    psum x1, blocking collectives, local(): sum_first, sum_second = lax.psum((local_first, local_second), 'space')  10.8 us
    dot_general x9, matrix products, local(): lax.dot_general(window, flat_cot, (((0,), (0,)), ((), ())), preferred_ele...  10.3 us
    slice x9, local copies, waits for them, and re-layouts, local(): cot_pad[2 - row_off:2 - row_off + height_dev, 2 - col_off:2 - col_off + w...  8.48 us
    psum x1, waiting for transfers between devices, local(): lax.psum(grad_piece.astype(jnp.bfloat16), 'space').astype(jnp.float32)  8.25 us
    slice x9, local copies, waits for them, and re-layouts, local(): act_pad[row_off:row_off + height_dev, col_off:col_off + width_dev]  7.27 us
    unnamed x45, local copies, waits for them, and re-layouts  6.36 us
  transfers between devices with their start and end apart: 6, of which 2 were waited for; matrix products, arithmetic and copies ran while one was open for 12% of the time, Pallas kernels for 0%

commit v1 on v0

--- a/solution.py
+++ b/solution.py
@@ -103,7 +103,9 @@
     local_second = group_sum(scaled * normed, GROUPS)
     grad_piece = lax.psum_scatter(weight_terms, "dp", scatter_dimension=0, tiled=True)
     sum_first, sum_second = lax.psum((local_first, local_second), "space")
-    grad_piece = lax.psum(grad_piece.astype(jnp.bfloat16), "space").astype(jnp.float32)
+    grad_piece = jnp.sum(
+        lax.all_gather(grad_piece.astype(jnp.bfloat16), axis_name="space"), axis=0
+    ).astype(jnp.float32)
     first = sum_first / cell_count
     second = sum_second / cell_count
     input_grad = (

time: 208 us -> 146 us (0.70)
  blocking collectives: 105 us -> 46.5 us
  matrix products: 20.9 us -> 15.4 us
  local copies, waits for them, and re-layouts: 36.4 us -> 39.1 us
  waiting for transfers between devices: 10.9 us -> 8.52 us
  starting transfers between devices: 6.8 us -> 9.12 us
    unnamed x1 -> x0, blocking collectives: 80.3 us -> none
    all_gather x0 -> x1, blocking collectives: none -> 21.9 us  [local(): lax.all_gather(grad_piece.astype(jnp.bfloat16), axis_name='space')]
    psum x1 -> x0, waiting for transfers between devices: 8.25 us -> none  [local(): lax.psum(grad_piece.astype(jnp.bfloat16), 'space').astype(jnp.float32)]
    unnamed x2 -> x3, waiting for transfers between devices: 0.54 us -> 8.5 us
    dot_general x9, matrix products: 10.3 us -> 3.19 us  [local(): lax.dot_general(window, flat_cot, (((0,), (0,)), ((), ())), preferred_ele...]
    reshape x1 -> x0, local copies, waits for them, and re-layouts: 5.63 us -> none  [local(): weight_terms = jnp.stack(tap_grads).reshape(9 * channels, channels)]
    unnamed x45 -> x58, local copies, waits for them, and re-layouts: 6.36 us -> 11.7 us
    ppermute x2, starting transfers between devices: 3.96 us -> 6.47 us  [with_halo(): lax.ppermute(tail, axis, [(i, (i + 1) % count) for i in range(ends)])]
  transfers between devices with their start and end apart: 6 -> 6, of which waited for: 2 -> 1; matrix products, arithmetic and copies ran while one was open for 12% -> 37% of each run, Pallas kernels for 0% -> 0%
where the time goes in v1:
time: 146 us; the launch traced here: 145 us
  blocking collectives  46.5 us (32%)
  local copies, waits for them, and re-layouts  39.1 us (27%)
  between operations  16.1 us (11%)
  matrix products  15.4 us (11%)
  other arithmetic  10.6 us (7%)
  starting transfers between devices  9.12 us (6%)
  waiting for transfers between devices  8.52 us (6%)
    all_gather x1, blocking collectives, local(): lax.all_gather(grad_piece.astype(jnp.bfloat16), axis_name='space')  21.9 us
    psum x1, blocking collectives, local(): lax.psum((group_sum(values, GROUPS), group_sum(values * values, GROUPS)),...  13.5 us
    unnamed x58, local copies, waits for them, and re-layouts  11.7 us
    psum x1, blocking collectives, local(): sum_first, sum_second = lax.psum((local_first, local_second), 'space')  11.1 us
    slice x9, local copies, waits for them, and re-layouts, local(): act_pad[row_off:row_off + height_dev, col_off:col_off + width_dev]  8.86 us
    unnamed x3, waiting for transfers between devices  8.5 us
    slice x9, local copies, waits for them, and re-layouts, local(): cot_pad[2 - row_off:2 - row_off + height_dev, 2 - col_off:2 - col_off + w...  7.56 us
    dot_general x9, matrix products, local(): lax.dot_general(cot_window, tap_weights[tap_index], (((1,), (1,)), ((), (...  7.1 us
  transfers between devices with their start and end apart: 6, of which 1 were waited for; matrix products, arithmetic and copies ran while one was open for 37% of the time, Pallas kernels for 0%

profile of v1, /device:TPU:0, one launch (start us, length us, event | category | flops | bytes accessed | tf_op | source)
XLA Modules:
  0.0 145.4 jit_solution(11671311081981444725)
XLA Ops:
  8.7 1.1 multiply_reduce_fusion.1
  10.3 13.5 %all-reduce.4 = (f32[32]{0:T(128)S(1)}, f32[32]{0:T(128)S(1)}) all-reduce(f32[32]{0:T(128)S(1)} %reduce_sum.62, f32[32]{0:T(128)S(1)} %reduce_sum.81), channel_id=1, replica_groups=mesh['space'=4,'dp'=8] {'space'}, use_global_device_ids=true, to_apply=%region_2.0 | all-reduce | flops 64 | bytes 512 | tf_op jit(solution)/shard_map/psum | solution.py:53
  24.2 1.3 multiply_convert_fusion.4
  25.5 1.3 collective-permute-start
  26.8 1.3 collective-permute-start.1
  28.2 1.0 bitcast_multiply_fusion.2
  29.9 5.2 %collective-permute-start.2 = (bf16[1,128,320]{1,2,0:T(8,128)(2,1)}, bf16[1,128,320]{1,2,0:T(8,128)(2,1)}, u32[]{:S(2)}, u32[]{:S(2)}) collective-permute-start(bf16[1,128,320]{1,2,0:T(8,128)(2,1)} %get-tuple-element.32), channel_id=1, source_target_pairs={{0,8},{8,16},{16,24},{1,9},{9,17},{17,25},{2,10},{10,18},{18,26},{... | collective-permute-start | bytes 245768 | tf_op jit(solution)/shard_map/ppermute | solution.py:17
  35.1 1.3 collective-permute-start.3
  37.9 2.1 %copy.69 = f32[360,320]{1,0:T(8,128)} copy(f32[360,320]{0,1:T(8,128)} %param.15) | data formatting | bytes 921600 | tf_op args[6]
  40.0 1.0 copy.47
  42.0 1.2 fusion.84
  43.2 1.2 copy.41
  47.9 2.0 %copy-done = f32[9,320,320]{2,1,0:T(8,128)} copy-done((f32[9,320,320]{2,1,0:T(8,128)}, f32[9,320,320]{2,1,0:T(8,128)S(1)}, u32[]{:S(2)}) %copy-start) | copy-done | bytes 3686424
  50.7 1.8 %copy.44 = bf16[3,128,320]{2,1,0:T(8,128)(2,1)} copy(bf16[3,128,320]{1,2,0:T(8,128)(2,1)} %get-tuple-element.28) | data formatting | bytes 491520 | tf_op jit(solution)/shard_map/slice | solution.py:66
  56.4 1.3 select_maximum_fusion
  59.0 1.0 pad_maximum_fusion
  66.3 4.2 %copy.42 = bf16[8,360,320]{1,0,2:T(8,128)(2,1)} copy(bf16[8,360,320]{1,2,0:T(8,128)(2,1)} %all-gather.5.cloned.1.call-done) | data formatting | bytes 3686400 | tf_op jit(solution)/shard_map/all_gather | solution.py:50
  70.6 3.5 %reshape.285 = bf16[2880,320]{0,1:T(8,128)(2,1)S(1)} reshape(bf16[8,360,320]{1,0,2:T(8,128)(2,1)} %copy.42) | data formatting | bytes 3686400
  74.4 1.3 fusion.50
  78.6 1.1 convolution_add_fusion.9
  79.7 1.3 copy.52
  80.9 1.0 copy.53
  82.0 1.5 %fusion.63 = f32[384,320]{0,1:T(8,128)S(1)} fusion(bf16[384,320]{1,0:T(8,128)(2,1)} %bitcast.155, bf16[2880,320]{0,1:T(8,128)(2,1)S(1)} %reshape.285), kind=kOutput, calls=%fused_computation.113 | convolution fusion | flops 78643200 | bytes 983040 | tf_op jit(solution)/shard_map/dot_general | solution.py:92
  83.4 1.5 %convolution_add_fusion.8 = f32[384,320]{0,1:T(8,128)S(1)} fusion(f32[384,320]{0,1:T(8,128)S(1)} %fusion.63, bf16[384,320]{1,0:T(8,128)(2,1)} %bitcast.159, bf16[2880,320]{0,1:T(8,128)(2,1)S(1)} %reshape.285), kind=kOutput, calls=%fused_computation.31 | convolution fusion | flops 78766080 | bytes 1474560 | tf_op jit(solution)/shard_map/dot_general | solution.py:92
  88.0 1.3 fusion.82
  89.8 11.1 %all-reduce.3 = (f32[32]{0:T(128)S(1)}, f32[32]{0:T(128)S(1)}) all-reduce(f32[32]{0:T(128)S(1)} %reduce_sum.87, f32[32]{0:T(128)S(1)} %reduce_sum.84), channel_id=1, replica_groups=mesh['space'=4,'dp'=8] {'space'}, use_global_device_ids=true, to_apply=%region_11.12 | all-reduce | flops 64 | bytes 512 | tf_op jit(solution)/shard_map/psum | solution.py:105
  101.3 1.3 copy.63
  102.8 1.3 multiply_convert_fusion.1
  104.1 8.5 %reduce-scatter.4.cloned.1.call-done = f32[360,320]{1,0:T(8,128)} async-done(((f32[2880,320]{1,0:T(8,128)}), f32[360,320]{1,0:T(8,128)}) %reduce-scatter.4.cloned.1.call-update) | async-done | bytes 460816
  112.6 1.1 convert_bitcast_fusion
  113.9 21.9 %all-gather.2 = bf16[4,360,320]{1,2,0:T(8,128)(2,1)S(1)} all-gather(bf16[1,360,320]{1,2,0:T(8,128)(2,1)S(1)} %copy.66), channel_id=2, replica_groups=mesh['space'=4,'dp'=8] {'space'}, dimensions={0}, use_global_device_ids=true | all-gather | bytes 1152000 | tf_op jit(solution)/shard_map/all_gather | solution.py:107
  137.6 1.0 copy.71
  (131 shorter events, 29.0 us)
Async XLA Ops:
  7.2 30.3 %copy-start.1 = (bf16[1,3,128,320]{2,3,1,0:T(8,128)(2,1)S(1)}, bf16[1,3,128,320]{2,3,1,0:T(8,128)(2,1)}, u32[]{:S(2)}) copy-start(bf16[1,3,128,320]{2,3,1,0:T(8,128)(2,1)} %param.9) | copy-start | bytes 737284
  7.2 29.2 %copy-start.15 = (bf16[1,3,128,320]{2,3,1,0:T(8,128)(2,1)S(1)}, bf16[1,3,128,320]{2,3,1,0:T(8,128)(2,1)}, u32[]{:S(2)}) copy-start(bf16[1,3,128,320]{2,3,1,0:T(8,128)(2,1)} %param.10) | copy-start | bytes 737284
  7.2 59.1 %all-gather.5.cloned.1.call-start = ((), (), s32[]{:S(2)}) async-start(), calls=%async_computation.1 | async-start | bytes 2211840 | tf_op jit(solution)/shard_map/all_gather | solution.py:50
  24.2 13.5 %copy-start.19 = (f32[360,320]{0,1:T(8,128)S(1)}, f32[360,320]{0,1:T(8,128)}, u32[]{:S(2)}) copy-start(f32[360,320]{0,1:T(8,128)} %param.14) | copy-start | bytes 1382404
  25.5 15.5 %collective-permute-start = (bf16[1,128,320]{1,2,0:T(8,128)(2,1)S(1)}, bf16[1,128,320]{1,2,0:T(8,128)(2,1)S(1)}, u32[]{:S(2)}, u32[]{:S(2)}) collective-permute-start(bf16[1,128,320]{1,2,0:T(8,128)(2,1)S(1)} %get-tuple-element.36), channel_id=1, source_target_pairs={{0,8},{8,16},{16,24},{1,9},{9,17},{17,25},{2,10},{10,18},{18,26},{... | collective-permute-start | bytes 245768 | tf_op jit(solution)/shard_map/ppermute | solution.py:17
  26.8 14.2 %collective-permute-start.1 = (bf16[1,128,320]{1,2,0:T(8,128)(2,1)S(1)}, bf16[1,128,320]{1,2,0:T(8,128)(2,1)S(1)}, u32[]{:S(2)}, u32[]{:S(2)}) collective-permute-start(bf16[1,128,320]{1,2,0:T(8,128)(2,1)S(1)} %get-tuple-element.37), channel_id=1, source_target_pairs={{8,0},{16,8},{24,16},{9,1},{17,9},{25,17},{10,2},{18,10},{26,18},{... | collective-permute-start | bytes 245768 | tf_op jit(solution)/shard_map/ppermute | solution.py:19
  28.2 84.4 %reduce-scatter.4.cloned.1.call-start = ((), (), s32[]{:S(2)}) async-start(), calls=%async_computation.2 | async-start | bytes 4976640
  29.9 26.5 %collective-permute-start.2 = (bf16[1,128,320]{1,2,0:T(8,128)(2,1)}, bf16[1,128,320]{1,2,0:T(8,128)(2,1)}, u32[]{:S(2)}, u32[]{:S(2)}) collective-permute-start(bf16[1,128,320]{1,2,0:T(8,128)(2,1)} %get-tuple-element.32), channel_id=1, source_target_pairs={{0,8},{8,16},{16,24},{1,9},{9,17},{17,25},{2,10},{10,18},{18,26},{... | collective-permute-start | bytes 245768 | tf_op jit(solution)/shard_map/ppermute | solution.py:17
  35.1 21.4 %collective-permute-start.3 = (bf16[1,128,320]{1,2,0:T(8,128)(2,1)}, bf16[1,128,320]{1,2,0:T(8,128)(2,1)}, u32[]{:S(2)}, u32[]{:S(2)}) collective-permute-start(bf16[1,128,320]{1,2,0:T(8,128)(2,1)} %get-tuple-element.33), channel_id=1, source_target_pairs={{8,0},{16,8},{24,16},{9,1},{17,9},{25,17},{10,2},{18,10},{26,18},{... | collective-permute-start | bytes 245768 | tf_op jit(solution)/shard_map/ppermute | solution.py:19
  41.0 0.6 copy-start.17
  44.4 1.4 copy-start.23
  44.4 1.4 copy-start.24
  46.2 0.9 copy-start.18
  47.1 5.4 %copy-start.16 = (bf16[3,128,320]{1,2,0:T(8,128)(2,1)S(1)}, bf16[3,128,320]{1,2,0:T(8,128)(2,1)}, u32[]{:S(2)}) copy-start(bf16[3,128,320]{1,2,0:T(8,128)(2,1)} %get-tuple-element.27) | copy-start | bytes 737284
  47.8 2.0 %copy-start = (f32[9,320,320]{2,1,0:T(8,128)}, f32[9,320,320]{2,1,0:T(8,128)S(1)}, u32[]{:S(2)}) copy-start(f32[9,320,320]{2,1,0:T(8,128)S(1)} %fusion.3) | copy-start | bytes 11059204
  74.1 1.7 %copy-start.9 = (bf16[3,128,320]{2,1,0:T(8,128)(2,1)S(1)}, bf16[3,128,320]{2,1,0:T(8,128)(2,1)}, u32[]{:S(2)}) copy-start(bf16[3,128,320]{2,1,0:T(8,128)(2,1)} %copy.48) | copy-start | bytes 737284
  74.1 2.1 %copy-start.8 = (bf16[3,128,320]{2,1,0:T(8,128)(2,1)S(1)}, bf16[3,128,320]{2,1,0:T(8,128)(2,1)}, u32[]{:S(2)}) copy-start(bf16[3,128,320]{2,1,0:T(8,128)(2,1)} %copy.43) | copy-start | bytes 737284
  74.4 2.2 %copy-start.7 = (bf16[3,128,320]{2,1,0:T(8,128)(2,1)S(1)}, bf16[3,128,320]{2,1,0:T(8,128)(2,1)}, u32[]{:S(2)}) copy-start(bf16[3,128,320]{2,1,0:T(8,128)(2,1)} %copy.44) | copy-start | bytes 737284
  75.8 1.1 copy-start.6
  76.6 1.1 copy-start.20
  77.6 1.0 copy-start.5
  81.9 3.0 %copy-start.14 = (bf16[3,128,320]{2,1,0:T(8,128)(2,1)S(1)}, bf16[3,128,320]{2,1,0:T(8,128)(2,1)}, u32[]{:S(2)}) copy-start(bf16[3,128,320]{2,1,0:T(8,128)(2,1)} %copy.56) | copy-start | bytes 737284
  81.9 3.4 %copy-start.13 = (bf16[3,128,320]{2,1,0:T(8,128)(2,1)S(1)}, bf16[3,128,320]{2,1,0:T(8,128)(2,1)}, u32[]{:S(2)}) copy-start(bf16[3,128,320]{2,1,0:T(8,128)(2,1)} %copy.57) | copy-start | bytes 737284
  85.0 1.0 copy-start.4
  85.4 1.0 copy-start.12
  85.9 1.0 copy-start.10
  86.3 1.0 copy-start.11
  86.9 1.1 copy-start.21
  86.9 1.1 copy-start.22
  89.4 13.4 %copy-start.3 = (f32[1,3,128,320]{2,3,1,0:T(8,128)S(1)}, f32[1,3,128,320]{2,3,1,0:T(8,128)}, u32[]{:S(2)}) copy-start(f32[1,3,128,320]{2,3,1,0:T(8,128)} %copy.53) | copy-start | bytes 1474564
  113.9 23.4 %copy-start.2 = (f32[360,320]{1,0:T(8,128)S(1)}, f32[360,320]{1,0:T(8,128)}, u32[]{:S(2)}) copy-start(f32[360,320]{1,0:T(8,128)} %copy.69) | copy-start | bytes 1382404
Sparse Core Ops, SparseCore 0:
  28.3 27.9 all-gather.4
  59.8 52.7 reduce-scatter.3
